TPU v7x, 256 devices: a whole 4x4x8 slice. The times are simulated.
256 devices in a mesh: seq: 64 (over x, z, core), head: 4 (over y).
Axes of the slice: x: 4, y: 4, z: 8, core: 2. Of those that a mesh axis runs over, the one named last changes fastest.
Arguments:
- acceptance_linear: bfloat16 [32768, 4096], P(('seq', 'head')), may hold values from -6 to 6
- lookup_linear: bfloat16 [32768, 4096], P(('seq', 'head')), may hold values from -6 to 6
- payload_linear: bfloat16 [32768, 4096], P(('seq', 'head')), may hold values from -6 to 6
- valve_linear: bfloat16 [32768, 4096], P(('seq', 'head')), may hold values from -6 to 6
- layer_entries: bfloat16 [32768, 4096], P(('seq', 'head')), may hold values from -6 to 6
- prompt_label: int32 [32768], replicated, may hold values from 0 to 15, never falling along the last dimension, each value on 1 to 8192 neighbouring positions
- fading_baseline: float32 [4096], replicated, may hold values from -12 to -3
- previous_mixing_share: float32 [4096], replicated, may hold values from 0.2 to 0.9
- fading_lower_map: bfloat16 [4096, 128], replicated, may hold values from -0.09375 to 0.09375
- fading_raise_map: bfloat16 [128, 4096], replicated, may hold values from -0.5 to 0.5
- diagonal_reward: float32 [4096], replicated, may hold values from -0.5 to 1
- cluster_gain_vector: float32 [4096], replicated, may hold values from 0.25 to 1.75
- cluster_mean_shift_add: float32 [4096], replicated, may hold values from -1.5 to 1.5
Outputs:
- gated: bfloat16 [32768, 4096], P(('seq', 'head'))
All inputs are finite; a program needn't handle non-finite values.
Results may differ from a plain program's by a relative error of at most 0.001.
The roundings to bfloat16 on the way count: a program that leaves them out, or rounds other values in their place, can miss the bound.
Values may be sent and summed in bfloat16 or wider, within the bound.
No kernel may reach another device: no remote copies, remote signals or barrier semaphores. Data moves between devices by JAX's collectives and lax.ppermute only.
A program may use at most 192 MiB of HBM per device.

v0:
```python
import jax
import jax.numpy as jnp
from jax import lax
from jax.sharding import PartitionSpec as P

ATTENTION_SPAN = 64
CH = 128
norm_eps = 0.00064
decay_floor = -0.5
highest = lax.Precision.HIGHEST


def shifted(value, axis, by):
    size = lax.axis_size(axis)
    pairs = [(i, i + by) for i in range(size) if 0 <= i + by < size]
    return lax.ppermute(value, axis, pairs)


def earlier_segment(prompt_label, position):
    earlier = lax.dynamic_slice_in_dim(prompt_label, jnp.maximum(position - 1, 0), 1, 0)
    return jnp.where(position > 0, earlier, jnp.full_like(earlier, -1))


def local(
    acceptance_linear,
    lookup_linear,
    payload_linear,
    valve_linear,
    layer_entries,
    prompt_label,
    fading_baseline,
    previous_mixing_share,
    fading_lower_map,
    fading_raise_map,
    diagonal_reward,
    cluster_gain_vector,
    cluster_mean_shift_add,
):
    head_count = lax.axis_size("head")
    seq_index = lax.axis_index("seq")
    head_index = lax.axis_index("head")
    row_count = layer_entries.shape[0]
    block_start = (seq_index * head_count + head_index) * row_count
    own_seg = lax.dynamic_slice_in_dim(prompt_label, block_start, row_count, 0)
    prior_seg = jnp.concatenate([earlier_segment(prompt_label, block_start), own_seg[:-1]])
    edge_row = shifted(layer_entries[-1:], ("seq", "head"), 1)
    prev_rows = jnp.concatenate([edge_row, layer_entries[:-1]], axis=0)
    prev_rows = jnp.where((prior_seg == own_seg)[:, None], prev_rows, jnp.zeros_like(prev_rows))
    current = layer_entries.astype(jnp.float32)
    blended_input = (
        current + (prev_rows.astype(jnp.float32) - current) * previous_mixing_share
    ).astype(jnp.bfloat16)
    decay_hidden_rows = jnp.tanh(
        jnp.dot(blended_input, fading_lower_map, preferred_element_type=jnp.float32)
    ).astype(jnp.bfloat16)
    decay_score = fading_baseline + jnp.dot(
        decay_hidden_rows, fading_raise_map, preferred_element_type=jnp.float32
    )
    log_decay = jnp.maximum(-jnp.exp(decay_score), decay_floor).astype(jnp.bfloat16)
    query_head, key_head, value_head, decay_head = (
        lax.all_to_all(acceptance_linear, "head", split_axis=1, concat_axis=0, tiled=True),
        lax.all_to_all(lookup_linear, "head", split_axis=1, concat_axis=0, tiled=True),
        lax.all_to_all(payload_linear, "head", split_axis=1, concat_axis=0, tiled=True),
        lax.all_to_all(log_decay, "head", split_axis=1, concat_axis=0, tiled=True),
    )
    tokens = query_head.shape[0]
    partition_extent = query_head.shape[1]
    local_heads = partition_extent // ATTENTION_SPAN
    stretches = tokens // CH
    seq_start = seq_index * tokens
    seg_block = lax.dynamic_slice_in_dim(prompt_label, seq_start, tokens, 0).reshape(stretches, CH)
    seg_before = earlier_segment(prompt_label, seq_start)
    stretch_prior = jnp.concatenate([seg_before, seg_block[:-1, -1]])
    feature_start = head_index * partition_extent
    partition_reward = lax.dynamic_slice_in_dim(
        diagonal_reward, feature_start, partition_extent, 0
    ).reshape(local_heads, ATTENTION_SPAN)
    gain_local = lax.dynamic_slice_in_dim(
        cluster_gain_vector, feature_start, partition_extent, 0
    ).reshape(local_heads, ATTENTION_SPAN)
    bias_local = lax.dynamic_slice_in_dim(
        cluster_mean_shift_add, feature_start, partition_extent, 0
    ).reshape(local_heads, ATTENTION_SPAN)
    blocked = (stretches, CH, local_heads, ATTENTION_SPAN)
    request_vectors = query_head.reshape(blocked).astype(jnp.float32)
    lookup_vectors = key_head.reshape(blocked).astype(jnp.float32)
    payload_vectors = value_head.reshape(blocked).astype(jnp.float32)
    decays = decay_head.reshape(blocked).astype(jnp.float32)
    cumulative = jnp.cumsum(decays, axis=1)
    before = cumulative - decays
    ending = cumulative[:, -1]
    scaled_query = request_vectors * jnp.exp(before)
    scaled_key = lookup_vectors * jnp.exp(-cumulative)
    scores = jnp.einsum("cthd,cshd->chts", scaled_query, scaled_key, precision=highest)
    causal = lax.broadcasted_iota(jnp.int32, (CH, CH), 0) > lax.broadcasted_iota(
        jnp.int32, (CH, CH), 1
    )
    allowed = causal[None] & (seg_block[:, :, None] == seg_block[:, None, :])
    scores = jnp.where(allowed[:, None], scores, jnp.zeros_like(scores))
    within = jnp.einsum("chts,cshd->cthd", scores, payload_vectors, precision=highest)
    diagonal_contribution = (
        jnp.sum(request_vectors * partition_reward * lookup_vectors, axis=3, keepdims=True)
        * payload_vectors
    )
    keep_last = (seg_block == seg_block[:, -1:]).astype(jnp.float32)
    tail_keys = lookup_vectors * jnp.exp(ending[:, None] - cumulative) * keep_last[:, :, None, None]
    stretch_state = jnp.einsum("cthd,cthe->chde", tail_keys, payload_vectors, precision=highest)
    stretch_decay = (
        jnp.exp(ending) * (seg_block[:, -1] == stretch_prior).astype(jnp.float32)[:, None, None]
    )

    def advance(carry_state, pieces):
        factor, new_part = pieces
        return (factor[:, :, None] * carry_state + new_part, carry_state)

    zero_state = jnp.zeros((local_heads, ATTENTION_SPAN, ATTENTION_SPAN), jnp.float32)
    span_state, local_start = lax.scan(advance, zero_state, (stretch_decay, stretch_state))

    def multiply(product, factor):
        return (product * factor, product)

    span_decay, decay_before = lax.scan(
        multiply, jnp.ones((local_heads, ATTENTION_SPAN), jnp.float32), stretch_decay
    )
    seq_count = lax.axis_size("seq")
    packed = jnp.concatenate([span_state, span_decay[:, None, :]], axis=1)

    def unpack(value):
        return (value[:, :ATTENTION_SPAN], value[:, ATTENTION_SPAN])

    prior_state, prior_decay = unpack(shifted(packed, "seq", 1))
    incoming, cover = (prior_state, prior_decay)
    reach = 1
    if seq_count > 2:
        far_state, far_decay = unpack(shifted(packed, "seq", 2))
        incoming = prior_decay[:, :, None] * far_state + prior_state
        cover = prior_decay * far_decay
        reach = 2
    while reach < seq_count - 1:
        far_state, far_decay = unpack(
            shifted(jnp.concatenate([incoming, cover[:, None, :]], axis=1), "seq", reach)
        )
        incoming = cover[:, :, None] * far_state + incoming
        cover = cover * far_decay
        reach *= 2
    start_state = local_start + decay_before[:, :, :, None] * incoming[None]
    keep_first = (seg_block == stretch_prior[:, None]).astype(jnp.float32)
    carried = jnp.einsum(
        "cthd,chde->cthe",
        scaled_query * keep_first[:, :, None, None],
        start_state,
        precision=highest,
    )
    mixing = within + diagonal_contribution + carried
    center = mixing - jnp.mean(mixing, axis=3, keepdims=True)
    spread = jnp.mean(center * center, axis=3, keepdims=True)
    normed = center * lax.rsqrt(spread + norm_eps) * gain_local + bias_local
    normed = normed.astype(jnp.bfloat16).reshape(tokens, partition_extent)
    returned = lax.all_to_all(normed, "head", split_axis=0, concat_axis=1, tiled=True)
    return (returned.astype(jnp.float32) * jax.nn.silu(valve_linear.astype(jnp.float32))).astype(
        jnp.bfloat16
    )


def solution(mesh):
    return jax.shard_map(
        local,
        mesh=mesh,
        in_specs=(
            P(("seq", "head"), None),
            P(("seq", "head"), None),
            P(("seq", "head"), None),
            P(("seq", "head"), None),
            P(("seq", "head"), None),
            P(),
            P(),
            P(),
            P(),
            P(),
            P(),
            P(),
            P(),
        ),
        out_specs=P(("seq", "head"), None),
        check_vma=False,
    )
```

profile of v0, /device:TPU:162, one launch (start us, length us, event | category | flops | bytes accessed | tf_op | source)
XLA Modules:
  0.0 318.2 jit_solution(3429438494521364704)
XLA Ops:
  2.4 4.5 %all-to-all-start = ((bf16[128,4,1024]{0,2,1:T(8,128)(2,1)}), bf16[128,4,1024]{0,2,1:T(8,128)(2,1)S(1)}, u32[]{:S(2)}, u32[]{:S(2)}) async-start(bf16[128,4,1024]{0,2,1:T(8,128)(2,1)} %bitcast.1), calls=%async_computation | async-start | bytes 2097152 | tf_op jit(solution)/shard_map/all_to_all | solution.py:61
  8.2 13.8 %all-to-all-done = bf16[128,4,1024]{0,2,1:T(8,128)(2,1)S(1)} async-done(((bf16[128,4,1024]{0,2,1:T(8,128)(2,1)}), bf16[128,4,1024]{0,2,1:T(8,128)(2,1)S(1)}, u32[]{:S(2)}, u32[]{:S(2)}) %all-to-all-start) | async-done | bytes 1048608 | tf_op jit(solution)/shard_map/all_to_all | solution.py:61
  22.0 3.5 %all-to-all-start.2 = ((bf16[128,4,1024]{0,2,1:T(8,128)(2,1)}), bf16[128,4,1024]{0,2,1:T(8,128)(2,1)S(1)}, u32[]{:S(2)}, u32[]{:S(2)}) async-start(bf16[128,4,1024]{0,2,1:T(8,128)(2,1)} %bitcast.88), calls=%async_computation.2 | async-start | bytes 2097152 | tf_op jit(solution)/shard_map/all_to_all | solution.py:62
  26.4 3.9 %collective-permute-start = (bf16[1,4096]{1,0:T(2,128)(2,1)S(1)}, bf16[1,4096]{1,0:T(2,128)(2,1)S(1)}, u32[]{:S(2)}, u32[]{:S(2)}) collective-permute-start(bf16[1,4096]{1,0:T(2,128)(2,1)S(1)} %slice.59), channel_id=1, source_target_pairs={{0,1},{1,2},{2,3},{3,4},{4,5},{5,6},{6,7},{7,8},{8,9},{9,10},{10,1... | collective-permute-start | bytes 24584 | tf_op jit(solution)/shard_map/ppermute | solution.py:16
  36.4 4.3 %fusion.4 = bf16[128,4096]{1,0:T(8,128)(2,1)} fusion(bf16[128,4096]{1,0:T(8,128)(2,1)S(1)} %copy-done, bf16[4096,128]{1,0:T(8,128)(2,1)} %param.25, bf16[128,4096]{1,0:T(8,128)(2,1)} %param.21, bf16[127,4096]{1,0:T(8,128)(2,1)} %bitcast.92, bf16[1,4096]{1,0:T(2,128)(2,1)S(1)} %collective-permute-done, f32[4096]{0:T(1024)S(1)} %copy-done.15, ...), kind=kOutput, calls=%fused_computation.10 | convolution fusion | flops 276316160 | bytes 5275776 | tf_op jit(solution)/shard_map/dot_general | solution.py:56
  43.1 5.5 %all-to-all-start.1 = ((bf16[128,4,1024]{0,2,1:T(8,128)(2,1)}), bf16[128,4,1024]{0,2,1:T(8,128)(2,1)}, u32[]{:S(2)}, u32[]{:S(2)}) async-start(bf16[128,4,1024]{0,2,1:T(8,128)(2,1)} %bitcast.5), calls=%async_computation.1 | async-start | bytes 2097152 | tf_op jit(solution)/shard_map/all_to_all | solution.py:64
  59.6 4.0 %copy.132 = f32[4,128,16,64]{3,2,1,0:T(8,128)} copy(f32[4,128,16,64]{1,3,2,0:T(8,128)} %bitcast.82) | data formatting | bytes 4194304 | tf_op jit(solution)/shard_map/convert_element_type | solution.py:86
  64.2 4.2 %all-to-all-start.3 = ((bf16[128,4,1024]{0,2,1:T(8,128)(2,1)}), bf16[128,4,1024]{0,2,1:T(8,128)(2,1)}, u32[]{:S(2)}, u32[]{:S(2)}) async-start(bf16[128,4,1024]{0,2,1:T(8,128)(2,1)} %bitcast.87), calls=%async_computation.3 | async-start | bytes 2097152 | tf_op jit(solution)/shard_map/all_to_all | solution.py:63
  71.2 4.1 %copy.128 = f32[4,128,16,64]{3,2,1,0:T(8,128)} copy(f32[4,128,16,64]{1,3,2,0:T(8,128)} %bitcast.84) | data formatting | bytes 4194304 | tf_op jit(solution)/shard_map/convert_element_type | solution.py:88
  80.4 11.3 %exponential_multiply_fusion = (f32[4,128,16,64]{3,2,1,0:T(8,128)}, f32[4,128,16,64]{3,2,1,0:T(8,128)}, f32[4,128,16,64]{3,2,1,0:T(8,128)}, f32[4,128,16,64]{3,2,1,0:T(8,128)}) fusion(f32[4,128,16,64]{3,2,1,0:T(8,128)} %copy.132, f32[4,128,16,64]{3,2,1,0:T(8,128)} %copy-done.3, f32[4,128]{1,0:T(4,128)S(1)} %get-tuple-element.125, ...), kind=kLoop, calls=%fused_computation.21 | loop fusion | flops 4194304 | bytes 16797696 | tf_op jit(solution)/shard_map/mul | solution.py:93
  91.8 7.8 %fusion.7 = f32[4,16,64,64]{3,2,1,0:T(8,128)} fusion(bf16[4,128,16,64]{1,3,2,0:T(8,128)(2,1)} %bitcast.14, f32[4,128,16,64]{3,2,1,0:T(8,128)} %get-tuple-element.120), kind=kOutput, calls=%fused_computation.13 | convolution fusion | flops 402653184 | bytes 4194304 | tf_op jit(solution)/shard_map/cthd,cthe->chde/dot_general | solution.py:107
  99.6 8.8 %while.26 = (s32[]{:T(128)}, f32[16,64,64]{2,1,0:T(8,128)S(1)}, f32[4,16,64,64]{3,2,1,0:T(8,128)}, f32[4,16,64]{2,1,0:T(8,128)S(1)}, f32[4,16,64,64]{3,2,1,0:T(8,128)}, /*index=5*/s32[]{:T(128)}, s32[]{:T(128)}) while((s32[]{:T(128)}, f32[16,64,64]{2,1,0:T(8,128)S(1)}, f32[4,16,64,64]{3,2,1,0:T(8,128)}, ...), condition=%wide.region_3.4_spmd.clone, body=%wide.region_2.3_spmd.clone.sunk | while | flops 262147 | bytes 1585260 | solution.py:117
  116.5 11.9 %collective-permute-done.2 = f32[16,65,64]{1,2,0:T(8,128)S(1)} collective-permute-done((f32[16,65,64]{1,2,0:T(8,128)}, f32[16,65,64]{1,2,0:T(8,128)S(1)}, u32[]{:S(2)}, u32[]{:S(2)}) %collective-permute-start.2) | collective-permute-done | bytes 266272 | tf_op jit(solution)/shard_map/ppermute | solution.py:16
  141.2 11.5 %collective-permute-done.3 = f32[16,65,64]{1,2,0:T(8,128)S(1)} collective-permute-done((f32[16,65,64]{1,2,0:T(8,128)S(1)}, f32[16,65,64]{1,2,0:T(8,128)S(1)}, u32[]{:S(2)}, u32[]{:S(2)}) %collective-permute-start.3) | collective-permute-done | bytes 266272 | tf_op jit(solution)/shard_map/ppermute | solution.py:16
  160.1 24.8 %collective-permute-done.4 = f32[16,65,64]{1,2,0:T(8,128)S(1)} collective-permute-done((f32[16,65,64]{1,2,0:T(8,128)S(1)}, f32[16,65,64]{1,2,0:T(8,128)S(1)}, u32[]{:S(2)}, u32[]{:S(2)}) %collective-permute-start.4) | collective-permute-done | bytes 266272 | tf_op jit(solution)/shard_map/ppermute | solution.py:16
  190.3 11.2 %collective-permute-start.5 = (f32[16,65,64]{1,2,0:T(8,128)}, f32[16,65,64]{1,2,0:T(8,128)S(1)}, u32[]{:S(2)}, u32[]{:S(2)}) collective-permute-start(f32[16,65,64]{1,2,0:T(8,128)} %pad_maximum_fusion.3), channel_id=1, source_target_pairs={{0,32},{4,36},{8,40},{12,44},{16,48},{20,52},{24,56},{28,60},{32,6... | collective-permute-start | bytes 798728 | tf_op jit(solution)/shard_map/ppermute | solution.py:16
  203.9 16.0 %collective-permute-done.5 = f32[16,65,64]{1,2,0:T(8,128)S(1)} collective-permute-done((f32[16,65,64]{1,2,0:T(8,128)}, f32[16,65,64]{1,2,0:T(8,128)S(1)}, u32[]{:S(2)}, u32[]{:S(2)}) %collective-permute-start.5) | collective-permute-done | bytes 266272 | tf_op jit(solution)/shard_map/ppermute | solution.py:16
  225.8 7.2 %collective-permute-start.6 = (f32[16,65,64]{1,2,0:T(8,128)S(1)}, f32[16,65,64]{1,2,0:T(8,128)S(1)}, u32[]{:S(2)}, u32[]{:S(2)}) collective-permute-start(f32[16,65,64]{1,2,0:T(8,128)S(1)} %pad_maximum_fusion.4), channel_id=1, source_target_pairs={{0,64},{4,68},{8,72},{12,76},{16,80},{20,84},{24,88},{28,92},{32,9... | collective-permute-start | bytes 798728 | tf_op jit(solution)/shard_map/ppermute | solution.py:16
  234.8 8.0 %collective-permute-done.6 = f32[16,65,64]{1,2,0:T(8,128)S(1)} collective-permute-done((f32[16,65,64]{1,2,0:T(8,128)S(1)}, f32[16,65,64]{1,2,0:T(8,128)S(1)}, u32[]{:S(2)}, u32[]{:S(2)}) %collective-permute-start.6) | collective-permute-done | bytes 266272 | tf_op jit(solution)/shard_map/ppermute | solution.py:16
  243.8 13.7 %collective-permute-start.7 = (f32[16,65,64]{1,2,0:T(8,128)S(1)}, f32[16,65,64]{1,2,0:T(8,128)S(1)}, u32[]{:S(2)}, u32[]{:S(2)}) collective-permute-start(f32[16,65,64]{1,2,0:T(8,128)S(1)} %pad_maximum_fusion.5), channel_id=1, source_target_pairs={{0,128},{4,132},{8,136},{12,140},{16,144},{20,148},{24,152},{28,15... | collective-permute-start | bytes 798728 | tf_op jit(solution)/shard_map/ppermute | solution.py:16
  257.5 16.5 %fusion.9 = f32[4,16,128,128]{3,2,1,0:T(8,128)} fusion(f32[4,128,16,64]{3,2,1,0:T(8,128)} %get-tuple-element.119, f32[4,128,16,64]{3,2,1,0:T(8,128)} %get-tuple-element.122), kind=kOutput, calls=%fused_computation.15 | convolution fusion | flops 805306368 | bytes 8388608 | tf_op jit(solution)/shard_map/cthd,cshd->chts/dot_general | solution.py:94
  274.3 10.6 %fusion.5 = f32[4,16,64,128]{3,2,1,0:T(8,128)S(1)} fusion(f32[4,128,16,64]{3,2,1,0:T(8,128)} %get-tuple-element.121, f32[4,16,64,64]{3,2,1,0:T(8,128)} %get-tuple-element.56, f32[16,64,64]{2,1,0:T(8,128)S(1)} %copy.151, f32[4,16,64]{2,1,0:T(8,128)S(1)} %get-tuple-element.57), kind=kOutput, calls=%fused_computation.11 | convolution fusion | flops 403177472 | bytes 5521408 | tf_op jit(solution)/shard_map/cthd,chde->cthe/dot_general | solution.py:148
  284.9 6.1 %fusion.56 = (f32[4,128,16]{1,2,0:T(8,128)S(1)}, f32[4,128,16,64]{1,3,2,0:T(8,128)S(1)}) fusion(f32[4,16,64,128]{3,2,1,0:T(8,128)S(1)} %fusion.5, f32[4,128,16,64]{1,3,2,0:T(8,128)S(1)} %copy-done.5, bf16[4,128,16,64]{1,3,2,0:T(8,128)(2,1)} %bitcast.14, f32[4,16,128,128]{3,2,1,0:T(8,128)S(1)} %copy-done.4, pred[4,128,128]{2,1,0:T(8,128)(4,1)S(1)} %compare_and_fusion), kind=kOutput, calls=%fused_computation.98 | convolution fusion | flops 808968192 | bytes 11632640 | tf_op jit(solution)/shard_map/chts,cshd->cthd/dot_general | solution.py:100
  292.1 18.4 %all_to_all.68 = bf16[4,128,1024]{1,2,0:T(8,128)(2,1)S(1)} all-to-all(bf16[4,128,1024]{1,2,0:T(8,128)(2,1)S(1)} %bitcast.86), channel_id=1, replica_groups=mesh['seq'=64,'head'=4] {'head'}, dimensions={0} | all-to-all | bytes 2097152 | tf_op jit(solution)/shard_map/all_to_all | solution.py:159
  (145 shorter events, 93.6 us)
Async XLA Ops:
  0.0 36.4 %copy-start = (bf16[128,4096]{1,0:T(8,128)(2,1)S(1)}, bf16[128,4096]{1,0:T(8,128)(2,1)}, u32[]{:S(2)}) copy-start(bf16[128,4096]{1,0:T(8,128)(2,1)} %param.26) | copy-start | bytes 3145732
  0.0 6.9 %copy-start.12 = (bf16[128,4096]{1,0:T(8,128)(2,1)S(1)}, bf16[128,4096]{1,0:T(8,128)(2,1)}, u32[]{:S(2)}) copy-start(bf16[128,4096]{1,0:T(8,128)(2,1)} %param.18) | copy-start | bytes 3145732
  2.4 19.6 %all-to-all-start = ((bf16[128,4,1024]{0,2,1:T(8,128)(2,1)}), bf16[128,4,1024]{0,2,1:T(8,128)(2,1)S(1)}, u32[]{:S(2)}, u32[]{:S(2)}) async-start(bf16[128,4,1024]{0,2,1:T(8,128)(2,1)} %bitcast.1), calls=%async_computation | async-start | bytes 2097152 | tf_op jit(solution)/shard_map/all_to_all | solution.py:61
  6.9 29.5 %copy-start.15 = (f32[4096]{0:T(1024)S(1)}, f32[4096]{0:T(1024)}, u32[]{:S(2)}) copy-start(f32[4096]{0:T(1024)} %param.24) | copy-start | bytes 49156
  6.9 29.5 %copy-start.16 = (f32[4096]{0:T(1024)S(1)}, f32[4096]{0:T(1024)}, u32[]{:S(2)}) copy-start(f32[4096]{0:T(1024)} %param.23) | copy-start | bytes 49156
  22.0 18.7 %copy-start.6 = (bf16[128,4,1024]{0,2,1:T(8,128)(2,1)}, bf16[128,4,1024]{0,2,1:T(8,128)(2,1)S(1)}, u32[]{:S(2)}) copy-start(bf16[128,4,1024]{0,2,1:T(8,128)(2,1)S(1)} %all-to-all-done) | copy-start | bytes 3145732
  22.0 21.1 %all-to-all-start.2 = ((bf16[128,4,1024]{0,2,1:T(8,128)(2,1)}), bf16[128,4,1024]{0,2,1:T(8,128)(2,1)S(1)}, u32[]{:S(2)}, u32[]{:S(2)}) async-start(bf16[128,4,1024]{0,2,1:T(8,128)(2,1)} %bitcast.88), calls=%async_computation.2 | async-start | bytes 2097152 | tf_op jit(solution)/shard_map/all_to_all | solution.py:62
  26.4 10.0 %collective-permute-start = (bf16[1,4096]{1,0:T(2,128)(2,1)S(1)}, bf16[1,4096]{1,0:T(2,128)(2,1)S(1)}, u32[]{:S(2)}, u32[]{:S(2)}) collective-permute-start(bf16[1,4096]{1,0:T(2,128)(2,1)S(1)} %slice.59), channel_id=1, source_target_pairs={{0,1},{1,2},{2,3},{3,4},{4,5},{5,6},{6,7},{7,8},{8,9},{9,10},{10,1... | collective-permute-start | bytes 24584 | tf_op jit(solution)/shard_map/ppermute | solution.py:16
  40.7 7.9 %copy-start.13 = (bf16[128,4096]{1,0:T(8,128)(2,1)S(1)}, bf16[128,4096]{1,0:T(8,128)(2,1)}, u32[]{:S(2)}) copy-start(bf16[128,4096]{1,0:T(8,128)(2,1)} %param.19) | copy-start | bytes 3145732
  43.1 5.5 %copy-start.7 = (bf16[128,4,1024]{0,2,1:T(8,128)(2,1)}, bf16[128,4,1024]{0,2,1:T(8,128)(2,1)S(1)}, u32[]{:S(2)}) copy-start(bf16[128,4,1024]{0,2,1:T(8,128)(2,1)S(1)} %all-to-all-done.2) | copy-start | bytes 3145732
  43.1 21.1 %all-to-all-start.1 = ((bf16[128,4,1024]{0,2,1:T(8,128)(2,1)}), bf16[128,4,1024]{0,2,1:T(8,128)(2,1)}, u32[]{:S(2)}, u32[]{:S(2)}) async-start(bf16[128,4,1024]{0,2,1:T(8,128)(2,1)} %bitcast.5), calls=%async_computation.1 | async-start | bytes 2097152 | tf_op jit(solution)/shard_map/all_to_all | solution.py:64
  64.2 27.6 %all-to-all-start.3 = ((bf16[128,4,1024]{0,2,1:T(8,128)(2,1)}), bf16[128,4,1024]{0,2,1:T(8,128)(2,1)}, u32[]{:S(2)}, u32[]{:S(2)}) async-start(bf16[128,4,1024]{0,2,1:T(8,128)(2,1)} %bitcast.87), calls=%async_computation.3 | async-start | bytes 2097152 | tf_op jit(solution)/shard_map/all_to_all | solution.py:63
  111.5 16.9 %collective-permute-start.2 = (f32[16,65,64]{1,2,0:T(8,128)}, f32[16,65,64]{1,2,0:T(8,128)S(1)}, u32[]{:S(2)}, u32[]{:S(2)}) collective-permute-start(f32[16,65,64]{1,2,0:T(8,128)} %pad_maximum_fusion), channel_id=1, source_target_pairs={{0,8},{4,12},{8,16},{12,20},{16,24},{20,28},{24,32},{28,36},{32,40... | collective-permute-start | bytes 798728 | tf_op jit(solution)/shard_map/ppermute | solution.py:16
  114.4 18.1 %collective-permute-start.1 = (f32[16,65,64]{1,2,0:T(8,128)}, f32[16,65,64]{1,2,0:T(8,128)S(1)}, u32[]{:S(2)}, u32[]{:S(2)}) collective-permute-start(f32[16,65,64]{1,2,0:T(8,128)} %pad_maximum_fusion), channel_id=1, source_target_pairs={{0,4},{4,8},{8,12},{12,16},{16,20},{20,24},{24,28},{28,32},{32,36}... | collective-permute-start | bytes 798728 | tf_op jit(solution)/shard_map/ppermute | solution.py:16
  132.6 3.3 %copy-start.10 = (f32[16,65,64]{1,2,0:T(8,128)}, f32[16,65,64]{1,2,0:T(8,128)S(1)}, u32[]{:S(2)}) copy-start(f32[16,65,64]{1,2,0:T(8,128)S(1)} %collective-permute-done.1) | copy-start | bytes 798724
  138.3 14.5 %collective-permute-start.3 = (f32[16,65,64]{1,2,0:T(8,128)S(1)}, f32[16,65,64]{1,2,0:T(8,128)S(1)}, u32[]{:S(2)}, u32[]{:S(2)}) collective-permute-start(f32[16,65,64]{1,2,0:T(8,128)S(1)} %pad_maximum_fusion.1), channel_id=1, source_target_pairs={{0,8},{4,12},{8,16},{12,20},{16,24},{20,28},{24,32},{28,36},{32,40... | collective-permute-start | bytes 798728 | tf_op jit(solution)/shard_map/ppermute | solution.py:16
  157.4 27.4 %collective-permute-start.4 = (f32[16,65,64]{1,2,0:T(8,128)S(1)}, f32[16,65,64]{1,2,0:T(8,128)S(1)}, u32[]{:S(2)}, u32[]{:S(2)}) collective-permute-start(f32[16,65,64]{1,2,0:T(8,128)S(1)} %pad_maximum_fusion.2), channel_id=1, source_target_pairs={{0,16},{4,20},{8,24},{12,28},{16,32},{20,36},{24,40},{28,44},{32,4... | collective-permute-start | bytes 798728 | tf_op jit(solution)/shard_map/ppermute | solution.py:16
  190.3 29.7 %collective-permute-start.5 = (f32[16,65,64]{1,2,0:T(8,128)}, f32[16,65,64]{1,2,0:T(8,128)S(1)}, u32[]{:S(2)}, u32[]{:S(2)}) collective-permute-start(f32[16,65,64]{1,2,0:T(8,128)} %pad_maximum_fusion.3), channel_id=1, source_target_pairs={{0,32},{4,36},{8,40},{12,44},{16,48},{20,52},{24,56},{28,60},{32,6... | collective-permute-start | bytes 798728 | tf_op jit(solution)/shard_map/ppermute | solution.py:16
  223.3 9.7 %copy-start.2 = (f32[128,4,1024]{0,2,1:T(8,128)S(1)}, f32[128,4,1024]{0,2,1:T(8,128)}, u32[]{:S(2)}) copy-start(f32[128,4,1024]{0,2,1:T(8,128)} %convert_element_type.114) | copy-start | bytes 6291460
  225.8 17.1 %collective-permute-start.6 = (f32[16,65,64]{1,2,0:T(8,128)S(1)}, f32[16,65,64]{1,2,0:T(8,128)S(1)}, u32[]{:S(2)}, u32[]{:S(2)}) collective-permute-start(f32[16,65,64]{1,2,0:T(8,128)S(1)} %pad_maximum_fusion.4), channel_id=1, source_target_pairs={{0,64},{4,68},{8,72},{12,76},{16,80},{20,84},{24,88},{28,92},{32,9... | collective-permute-start | bytes 798728 | tf_op jit(solution)/shard_map/ppermute | solution.py:16
  243.8 30.2 %collective-permute-start.7 = (f32[16,65,64]{1,2,0:T(8,128)S(1)}, f32[16,65,64]{1,2,0:T(8,128)S(1)}, u32[]{:S(2)}, u32[]{:S(2)}) collective-permute-start(f32[16,65,64]{1,2,0:T(8,128)S(1)} %pad_maximum_fusion.5), channel_id=1, source_target_pairs={{0,128},{4,132},{8,136},{12,140},{16,144},{20,148},{24,152},{28,15... | collective-permute-start | bytes 798728 | tf_op jit(solution)/shard_map/ppermute | solution.py:16
  274.3 10.6 %copy-start.4 = (f32[4,16,128,128]{3,2,1,0:T(8,128)S(1)}, f32[4,16,128,128]{3,2,1,0:T(8,128)}, u32[]{:S(2)}) copy-start(f32[4,16,128,128]{3,2,1,0:T(8,128)} %fusion.9) | copy-start | bytes 12582916
  274.3 10.6 %copy-start.5 = (f32[4,128,16,64]{1,3,2,0:T(8,128)S(1)}, f32[4,128,16,64]{1,3,2,0:T(8,128)}, u32[]{:S(2)}) copy-start(f32[4,128,16,64]{1,3,2,0:T(8,128)} %fusion) | copy-start | bytes 6291460
  312.0 6.2 %copy-start.1 = (bf16[128,4096]{1,0:T(8,128)(2,1)S(1)}, bf16[128,4096]{1,0:T(8,128)(2,1)}, u32[]{:S(2)}) copy-start(bf16[128,4096]{1,0:T(8,128)(2,1)} %param.26) | copy-start | bytes 3145732
  (5 other events, 10.1 us)
where the time goes:
time: 320 us; the launch traced here: 318 us
  waiting for transfers between devices  90.9 us (28%)
  starting transfers between devices  64.3 us (20%)
  other arithmetic  51.7 us (16%)
  local copies, waits for them, and re-layouts  45.7 us (14%)
  matrix products  45.2 us (14%)
  blocking collectives  18.4 us (6%)
    ppermute x8, waiting for transfers between devices, shifted(): return lax.ppermute(value, axis, pairs)  76.6 us
    ppermute x8, starting transfers between devices, shifted(): return lax.ppermute(value, axis, pairs)  46.5 us
    all_to_all x1, blocking collectives, local(): lax.all_to_all(normed, 'head', split_axis=0, concat_axis=1, tiled=True)  18.4 us
    dot_general x1, matrix products, local(): jnp.einsum('cthd,cshd->chts', scaled_query, scaled_key, precision=highest)  16.5 us
    all_to_all x1, waiting for transfers between devices, local(): lax.all_to_all(acceptance_linear, 'head', split_axis=1, concat_axis=0, ti...  13.8 us
    unnamed x42, local copies, waits for them, and re-layouts  11.8 us
    mul x1, other arithmetic, local(): scaled_key = lookup_vectors * jnp.exp(-cumulative)  11.3 us
    dot_general x1, matrix products, local(): jnp.einsum('cthd,chde->cthe', scaled_query * keep_first[:, :, None, None]...  10.6 us
  transfers between devices with their start and end apart: 12, of which 9 were waited for; matrix products, arithmetic and copies ran while one was open for 22% of the time, Pallas kernels for 0%

commit v1 on v0

--- a/solution.py
+++ b/solution.py
@@ -58,7 +58,12 @@
     )
     log_decay = jnp.maximum(-jnp.exp(decay_score), decay_floor).astype(jnp.bfloat16)
     query_head, key_head, value_head, decay_head = (
-        lax.all_to_all(acceptance_linear, "head", split_axis=1, concat_axis=0, tiled=True),
+        jnp.concatenate(
+            lax.all_to_all(
+                jnp.stack(jnp.split(acceptance_linear, lax.axis_size("head"), axis=1)), "head", 0, 0
+            ),
+            axis=0,
+        ),
         lax.all_to_all(lookup_linear, "head", split_axis=1, concat_axis=0, tiled=True),
         lax.all_to_all(payload_linear, "head", split_axis=1, concat_axis=0, tiled=True),
         lax.all_to_all(log_decay, "head", split_axis=1, concat_axis=0, tiled=True),

time: 320 us -> 320 us (level)
  the two profiles are of different devices: /device:TPU:162 before, /device:TPU:2 now
where the time goes in v1:
time: 320 us; the launch traced here: 318 us
  waiting for transfers between devices  108 us (34%)
  local copies, waits for them, and re-layouts  52.9 us (17%)
  other arithmetic  48.1 us (15%)
  matrix products  44.2 us (14%)
  starting transfers between devices  43.8 us (14%)
  blocking collectives  18.7 us (6%)
    ppermute x8, waiting for transfers between devices, shifted(): return lax.ppermute(value, axis, pairs)  95.1 us
    ppermute x8, starting transfers between devices, shifted(): return lax.ppermute(value, axis, pairs)  26 us
    all_to_all x1, blocking collectives, local(): lax.all_to_all(normed, 'head', split_axis=0, concat_axis=1, tiled=True)  18.7 us
    unnamed x57, local copies, waits for them, and re-layouts  17.9 us
    dot_general x1, matrix products, local(): jnp.einsum('cthd,cshd->chts', scaled_query, scaled_key, precision=highest)  16.4 us
    dot_general x1, matrix products, local(): jnp.einsum('cthd,chde->cthe', scaled_query * keep_first[:, :, None, None]...  10.3 us
    all_to_all x1, waiting for transfers between devices, local(): lax.all_to_all(lookup_linear, 'head', split_axis=1, concat_axis=0, tiled=...  9.45 us
    mul x1, other arithmetic, local(): scaled_key = lookup_vectors * jnp.exp(-cumulative)  8.27 us
  transfers between devices with their start and end apart: 12, of which 9 were waited for; matrix products, arithmetic and copies ran while one was open for 21% of the time, Pallas kernels for 0%

profile of v1, /device:TPU:2, one launch (start us, length us, event | category | flops | bytes accessed | tf_op | source)
XLA Modules:
  0.0 317.8 jit_solution(11915021360664976711)
XLA Ops:
  2.4 4.5 %all-to-all-start.2 = ((bf16[128,4,1024]{0,2,1:T(8,128)(2,1)}), bf16[128,4,1024]{0,2,1:T(8,128)(2,1)S(1)}, u32[]{:S(2)}, u32[]{:S(2)}) async-start(bf16[128,4,1024]{0,2,1:T(8,128)(2,1)} %bitcast.11), calls=%async_computation.2 | async-start | bytes 2097152 | tf_op jit(solution)/shard_map/all_to_all | solution.py:67
  12.5 9.5 %all-to-all-done.2 = bf16[128,4,1024]{0,2,1:T(8,128)(2,1)S(1)} async-done(((bf16[128,4,1024]{0,2,1:T(8,128)(2,1)}), bf16[128,4,1024]{0,2,1:T(8,128)(2,1)S(1)}, u32[]{:S(2)}, u32[]{:S(2)}) %all-to-all-start.2) | async-done | bytes 1048608 | tf_op jit(solution)/shard_map/all_to_all | solution.py:67
  26.5 3.9 %collective-permute-start = (bf16[1,4096]{1,0:T(2,128)(2,1)S(1)}, bf16[1,4096]{1,0:T(2,128)(2,1)S(1)}, u32[]{:S(2)}, u32[]{:S(2)}) collective-permute-start(bf16[1,4096]{1,0:T(2,128)(2,1)S(1)} %slice.59), channel_id=1, source_target_pairs={{0,1},{1,2},{2,3},{3,4},{4,5},{5,6},{6,7},{7,8},{8,9},{9,10},{10,1... | collective-permute-start | bytes 24584 | tf_op jit(solution)/shard_map/ppermute | solution.py:16
  43.3 5.5 %all-to-all-start.1 = ((bf16[128,4,1024]{0,2,1:T(8,128)(2,1)}), bf16[128,4,1024]{0,2,1:T(8,128)(2,1)}, u32[]{:S(2)}, u32[]{:S(2)}) async-start(bf16[128,4,1024]{0,2,1:T(8,128)(2,1)} %bitcast.7), calls=%async_computation.1 | async-start | bytes 2097152 | tf_op jit(solution)/shard_map/all_to_all | solution.py:69
  57.0 3.6 %copy.141 = f32[4,128,16,64]{3,2,1,0:T(8,128)} copy(bf16[4,128,16,64]{1,3,2,0:T(8,128)(2,1)} %bitcast.84) | data formatting | bytes 3145728 | tf_op jit(solution)/shard_map/convert_element_type | solution.py:90
  60.6 3.8 %all-to-all-done.1 = bf16[128,4,1024]{0,2,1:T(8,128)(2,1)} async-done(((bf16[128,4,1024]{0,2,1:T(8,128)(2,1)}), bf16[128,4,1024]{0,2,1:T(8,128)(2,1)}, u32[]{:S(2)}, u32[]{:S(2)}) %all-to-all-start.1) | async-done | bytes 1048608 | tf_op jit(solution)/shard_map/all_to_all | solution.py:69
  64.5 4.3 %all-to-all-start.3 = ((bf16[128,4,1024]{0,2,1:T(8,128)(2,1)}), bf16[128,4,1024]{0,2,1:T(8,128)(2,1)}, u32[]{:S(2)}, u32[]{:S(2)}) async-start(bf16[128,4,1024]{0,2,1:T(8,128)(2,1)} %bitcast.89), calls=%async_computation.3 | async-start | bytes 2097152 | tf_op jit(solution)/shard_map/all_to_all | solution.py:68
  71.5 4.1 %copy.139 = f32[4,128,16,64]{3,2,1,0:T(8,128)} copy(f32[4,128,16,64]{1,3,2,0:T(8,128)} %bitcast.86) | data formatting | bytes 4194304 | tf_op jit(solution)/shard_map/convert_element_type | solution.py:93
  80.3 8.3 %exponential_multiply_fusion = (f32[4,128,16,64]{3,2,1,0:T(8,128)}, f32[4,128,16,64]{3,2,1,0:T(8,128)}, f32[4,128,16,64]{3,2,1,0:T(8,128)}, f32[4,128,16,64]{3,2,1,0:T(8,128)}) fusion(f32[4,128,16,64]{3,2,1,0:T(8,128)} %copy.143, f32[4,128,16,64]{3,2,1,0:T(8,128)S(1)} %fusion.59, f32[4,128]{1,0:T(4,128)S(1)} %get-tuple-element.129, ...), kind=kLoop, calls=%fused_computation.21 | loop fusion | flops 4194304 | bytes 16797696 | tf_op jit(solution)/shard_map/mul | solution.py:98
  88.5 7.8 %fusion.7 = f32[4,16,64,64]{3,2,1,0:T(8,128)} fusion(bf16[4,128,16,64]{1,3,2,0:T(8,128)(2,1)} %bitcast.16, f32[4,128,16,64]{3,2,1,0:T(8,128)} %get-tuple-element.120), kind=kOutput, calls=%fused_computation.13 | convolution fusion | flops 402653184 | bytes 4194304 | tf_op jit(solution)/shard_map/cthd,cthe->chde/dot_general | solution.py:112
  96.3 8.9 %while.26 = (s32[]{:T(128)}, f32[16,64,64]{2,1,0:T(8,128)S(1)}, f32[4,16,64,64]{3,2,1,0:T(8,128)}, f32[4,16,64]{2,1,0:T(8,128)S(1)}, f32[4,16,64,64]{3,2,1,0:T(8,128)}, /*index=5*/s32[]{:T(128)}, s32[]{:T(128)}) while((s32[]{:T(128)}, f32[16,64,64]{2,1,0:T(8,128)S(1)}, f32[4,16,64,64]{3,2,1,0:T(8,128)}, ...), condition=%wide.region_3.4_spmd.clone, body=%wide.region_2.3_spmd.clone.sunk | while | flops 262147 | bytes 1585260 | solution.py:122
  110.6 4.0 %collective-permute-start.2 = (f32[16,65,64]{1,2,0:T(8,128)}, f32[16,65,64]{1,2,0:T(8,128)S(1)}, u32[]{:S(2)}, u32[]{:S(2)}) collective-permute-start(f32[16,65,64]{1,2,0:T(8,128)} %pad_maximum_fusion.1), channel_id=1, source_target_pairs={{0,8},{4,12},{8,16},{12,20},{16,24},{20,28},{24,32},{28,36},{32,40... | collective-permute-start | bytes 798728 | tf_op jit(solution)/shard_map/ppermute | solution.py:16
  114.6 9.6 %collective-permute-done.1 = f32[16,65,64]{1,2,0:T(8,128)S(1)} collective-permute-done((f32[16,65,64]{1,2,0:T(8,128)}, f32[16,65,64]{1,2,0:T(8,128)S(1)}, u32[]{:S(2)}, u32[]{:S(2)}) %collective-permute-start.1) | collective-permute-done | bytes 266272 | tf_op jit(solution)/shard_map/ppermute | solution.py:16
  126.4 5.1 %collective-permute-done.2 = f32[16,65,64]{1,2,0:T(8,128)S(1)} collective-permute-done((f32[16,65,64]{1,2,0:T(8,128)}, f32[16,65,64]{1,2,0:T(8,128)S(1)}, u32[]{:S(2)}, u32[]{:S(2)}) %collective-permute-start.2) | collective-permute-done | bytes 266272 | tf_op jit(solution)/shard_map/ppermute | solution.py:16
  139.2 16.0 %collective-permute-done.3 = f32[16,65,64]{1,2,0:T(8,128)S(1)} collective-permute-done((f32[16,65,64]{1,2,0:T(8,128)S(1)}, f32[16,65,64]{1,2,0:T(8,128)S(1)}, u32[]{:S(2)}, u32[]{:S(2)}) %collective-permute-start.3) | collective-permute-done | bytes 266272 | tf_op jit(solution)/shard_map/ppermute | solution.py:16
  162.9 26.6 %collective-permute-done.4 = f32[16,65,64]{1,2,0:T(8,128)S(1)} collective-permute-done((f32[16,65,64]{1,2,0:T(8,128)S(1)}, f32[16,65,64]{1,2,0:T(8,128)S(1)}, u32[]{:S(2)}, u32[]{:S(2)}) %collective-permute-start.4) | collective-permute-done | bytes 266272 | tf_op jit(solution)/shard_map/ppermute | solution.py:16
  196.2 4.6 %collective-permute-start.5 = (f32[16,65,64]{1,2,0:T(8,128)}, f32[16,65,64]{1,2,0:T(8,128)S(1)}, u32[]{:S(2)}, u32[]{:S(2)}) collective-permute-start(f32[16,65,64]{1,2,0:T(8,128)} %pad_maximum_fusion.4), channel_id=1, source_target_pairs={{0,32},{4,36},{8,40},{12,44},{16,48},{20,52},{24,56},{28,60},{32,6... | collective-permute-start | bytes 798728 | tf_op jit(solution)/shard_map/ppermute | solution.py:16
  203.2 23.9 %collective-permute-done.5 = f32[16,65,64]{1,2,0:T(8,128)S(1)} collective-permute-done((f32[16,65,64]{1,2,0:T(8,128)}, f32[16,65,64]{1,2,0:T(8,128)S(1)}, u32[]{:S(2)}, u32[]{:S(2)}) %collective-permute-start.5) | collective-permute-done | bytes 266272 | tf_op jit(solution)/shard_map/ppermute | solution.py:16
  240.0 10.5 %collective-permute-done.6 = f32[16,65,64]{1,2,0:T(8,128)S(1)} collective-permute-done((f32[16,65,64]{1,2,0:T(8,128)S(1)}, f32[16,65,64]{1,2,0:T(8,128)S(1)}, u32[]{:S(2)}, u32[]{:S(2)}) %collective-permute-start.6) | collective-permute-done | bytes 266272 | tf_op jit(solution)/shard_map/ppermute | solution.py:16
  253.3 4.3 %collective-permute-start.7 = (f32[16,65,64]{1,2,0:T(8,128)S(1)}, f32[16,65,64]{1,2,0:T(8,128)S(1)}, u32[]{:S(2)}, u32[]{:S(2)}) collective-permute-start(f32[16,65,64]{1,2,0:T(8,128)S(1)} %pad_maximum_fusion.6), channel_id=1, source_target_pairs={{0,128},{4,132},{8,136},{12,140},{16,144},{20,148},{24,152},{28,15... | collective-permute-start | bytes 798728 | tf_op jit(solution)/shard_map/ppermute | solution.py:16
  257.6 16.4 %fusion.9 = f32[4,16,128,128]{3,2,1,0:T(8,128)} fusion(f32[4,128,16,64]{3,2,1,0:T(8,128)} %get-tuple-element.119, f32[4,128,16,64]{3,2,1,0:T(8,128)} %get-tuple-element.122), kind=kOutput, calls=%fused_computation.15 | convolution fusion | flops 805306368 | bytes 8388608 | tf_op jit(solution)/shard_map/cthd,cshd->chts/dot_general | solution.py:99
  276.1 10.3 %fusion.5 = f32[4,16,64,128]{3,2,1,0:T(8,128)S(1)} fusion(f32[4,128,16,64]{3,2,1,0:T(8,128)} %get-tuple-element.121, f32[4,16,64,64]{3,2,1,0:T(8,128)S(1)} %copy-done.12, f32[16,64,64]{2,1,0:T(8,128)S(1)} %copy.162, f32[4,16,64]{2,1,0:T(8,128)S(1)} %get-tuple-element.57), kind=kOutput, calls=%fused_computation.11 | convolution fusion | flops 403177472 | bytes 5521408 | tf_op jit(solution)/shard_map/cthd,chde->cthe/dot_general | solution.py:153
  286.4 6.1 %fusion.58 = (f32[4,128,16]{1,2,0:T(8,128)S(1)}, f32[4,128,16,64]{1,3,2,0:T(8,128)S(1)}) fusion(f32[4,16,64,128]{3,2,1,0:T(8,128)S(1)} %fusion.5, f32[4,128,16,64]{1,3,2,0:T(8,128)S(1)} %copy-done.7, bf16[4,128,16,64]{1,3,2,0:T(8,128)(2,1)} %bitcast.16, f32[4,16,128,128]{3,2,1,0:T(8,128)S(1)} %copy-done.4, pred[4,128,128]{2,1,0:T(8,128)(4,1)S(1)} %compare_and_fusion), kind=kOutput, calls=%fused_computation.101 | convolution fusion | flops 808968192 | bytes 11632640 | tf_op jit(solution)/shard_map/chts,cshd->cthd/dot_general | solution.py:105
  293.7 18.7 %all_to_all.60 = bf16[4,128,1024]{1,2,0:T(8,128)(2,1)S(1)} all-to-all(bf16[4,128,1024]{1,2,0:T(8,128)(2,1)S(1)} %bitcast.88), channel_id=1, replica_groups=mesh['seq'=64,'head'=4] {'head'}, dimensions={0} | all-to-all | bytes 2097152 | tf_op jit(solution)/shard_map/all_to_all | solution.py:164
  (161 shorter events, 105.0 us)
Async XLA Ops:
  0.0 37.4 %copy-start = (bf16[128,4096]{1,0:T(8,128)(2,1)S(1)}, bf16[128,4096]{1,0:T(8,128)(2,1)}, u32[]{:S(2)}) copy-start(bf16[128,4096]{1,0:T(8,128)(2,1)} %param.26) | copy-start | bytes 3145732
  0.0 6.9 %copy-start.18 = (bf16[128,4096]{1,0:T(8,128)(2,1)S(1)}, bf16[128,4096]{1,0:T(8,128)(2,1)}, u32[]{:S(2)}) copy-start(bf16[128,4096]{1,0:T(8,128)(2,1)} %param.17) | copy-start | bytes 3145732
  2.4 19.6 %all-to-all-start.2 = ((bf16[128,4,1024]{0,2,1:T(8,128)(2,1)}), bf16[128,4,1024]{0,2,1:T(8,128)(2,1)S(1)}, u32[]{:S(2)}, u32[]{:S(2)}) async-start(bf16[128,4,1024]{0,2,1:T(8,128)(2,1)} %bitcast.11), calls=%async_computation.2 | async-start | bytes 2097152 | tf_op jit(solution)/shard_map/all_to_all | solution.py:67
  11.4 26.0 %copy-start.21 = (f32[4096]{0:T(1024)S(1)}, f32[4096]{0:T(1024)}, u32[]{:S(2)}) copy-start(f32[4096]{0:T(1024)} %param.24) | copy-start | bytes 49156
  11.4 26.0 %copy-start.22 = (f32[4096]{0:T(1024)S(1)}, f32[4096]{0:T(1024)}, u32[]{:S(2)}) copy-start(f32[4096]{0:T(1024)} %param.23) | copy-start | bytes 49156
  12.5 14.0 %copy-start.20 = (bf16[128,4096]{1,0:T(8,128)(2,1)S(1)}, bf16[128,4096]{1,0:T(8,128)(2,1)}, u32[]{:S(2)}) copy-start(bf16[128,4096]{1,0:T(8,128)(2,1)} %param.21) | copy-start | bytes 3145732
  22.9 20.4 %all-to-all-start = ((bf16[4,128,1024]{1,2,0:T(8,128)(2,1)}), bf16[4,128,1024]{1,2,0:T(8,128)(2,1)S(1)}, u32[]{:S(2)}, u32[]{:S(2)}) async-start(bf16[4,128,1024]{1,2,0:T(8,128)(2,1)} %pad_maximum_fusion), calls=%async_computation | async-start | bytes 2097152 | tf_op jit(solution)/shard_map/all_to_all | solution.py:62
  26.5 10.9 %collective-permute-start = (bf16[1,4096]{1,0:T(2,128)(2,1)S(1)}, bf16[1,4096]{1,0:T(2,128)(2,1)S(1)}, u32[]{:S(2)}, u32[]{:S(2)}) collective-permute-start(bf16[1,4096]{1,0:T(2,128)(2,1)S(1)} %slice.59), channel_id=1, source_target_pairs={{0,1},{1,2},{2,3},{3,4},{4,5},{5,6},{6,7},{7,8},{8,9},{9,10},{10,1... | collective-permute-start | bytes 24584 | tf_op jit(solution)/shard_map/ppermute | solution.py:16
  41.0 7.8 %copy-start.19 = (bf16[128,4096]{1,0:T(8,128)(2,1)S(1)}, bf16[128,4096]{1,0:T(8,128)(2,1)}, u32[]{:S(2)}) copy-start(bf16[128,4096]{1,0:T(8,128)(2,1)} %param.19) | copy-start | bytes 3145732
  43.3 6.8 %copy-start.5 = (bf16[4,128,1024]{1,2,0:T(8,128)(2,1)}, bf16[4,128,1024]{1,2,0:T(8,128)(2,1)S(1)}, u32[]{:S(2)}) copy-start(bf16[4,128,1024]{1,2,0:T(8,128)(2,1)S(1)} %all-to-all-done) | copy-start | bytes 3145732
  43.3 21.1 %all-to-all-start.1 = ((bf16[128,4,1024]{0,2,1:T(8,128)(2,1)}), bf16[128,4,1024]{0,2,1:T(8,128)(2,1)}, u32[]{:S(2)}, u32[]{:S(2)}) async-start(bf16[128,4,1024]{0,2,1:T(8,128)(2,1)} %bitcast.7), calls=%async_computation.1 | async-start | bytes 2097152 | tf_op jit(solution)/shard_map/all_to_all | solution.py:69
  64.5 24.1 %all-to-all-start.3 = ((bf16[128,4,1024]{0,2,1:T(8,128)(2,1)}), bf16[128,4,1024]{0,2,1:T(8,128)(2,1)}, u32[]{:S(2)}, u32[]{:S(2)}) async-start(bf16[128,4,1024]{0,2,1:T(8,128)(2,1)} %bitcast.89), calls=%async_computation.3 | async-start | bytes 2097152 | tf_op jit(solution)/shard_map/all_to_all | solution.py:68
  108.7 15.5 %collective-permute-start.1 = (f32[16,65,64]{1,2,0:T(8,128)}, f32[16,65,64]{1,2,0:T(8,128)S(1)}, u32[]{:S(2)}, u32[]{:S(2)}) collective-permute-start(f32[16,65,64]{1,2,0:T(8,128)} %pad_maximum_fusion.1), channel_id=1, source_target_pairs={{0,4},{4,8},{8,12},{12,16},{16,20},{20,24},{24,28},{28,32},{32,36}... | collective-permute-start | bytes 798728 | tf_op jit(solution)/shard_map/ppermute | solution.py:16
  110.6 20.9 %collective-permute-start.2 = (f32[16,65,64]{1,2,0:T(8,128)}, f32[16,65,64]{1,2,0:T(8,128)S(1)}, u32[]{:S(2)}, u32[]{:S(2)}) collective-permute-start(f32[16,65,64]{1,2,0:T(8,128)} %pad_maximum_fusion.1), channel_id=1, source_target_pairs={{0,8},{4,12},{8,16},{12,20},{16,24},{20,28},{24,32},{28,36},{32,40... | collective-permute-start | bytes 798728 | tf_op jit(solution)/shard_map/ppermute | solution.py:16
  137.2 18.0 %collective-permute-start.3 = (f32[16,65,64]{1,2,0:T(8,128)S(1)}, f32[16,65,64]{1,2,0:T(8,128)S(1)}, u32[]{:S(2)}, u32[]{:S(2)}) collective-permute-start(f32[16,65,64]{1,2,0:T(8,128)S(1)} %pad_maximum_fusion.2), channel_id=1, source_target_pairs={{0,8},{4,12},{8,16},{12,20},{16,24},{20,28},{24,32},{28,36},{32,40... | collective-permute-start | bytes 798728 | tf_op jit(solution)/shard_map/ppermute | solution.py:16
  161.0 28.5 %collective-permute-start.4 = (f32[16,65,64]{1,2,0:T(8,128)S(1)}, f32[16,65,64]{1,2,0:T(8,128)S(1)}, u32[]{:S(2)}, u32[]{:S(2)}) collective-permute-start(f32[16,65,64]{1,2,0:T(8,128)S(1)} %pad_maximum_fusion.3), channel_id=1, source_target_pairs={{0,16},{4,20},{8,24},{12,28},{16,32},{20,36},{24,40},{28,44},{32,4... | collective-permute-start | bytes 798728 | tf_op jit(solution)/shard_map/ppermute | solution.py:16
  194.0 33.2 %copy-start.8 = (f32[16,64,64]{1,2,0:T(8,128)}, f32[16,64,64]{1,2,0:T(8,128)S(1)}, u32[]{:S(2)}) copy-start(f32[16,64,64]{1,2,0:T(8,128)S(1)} %fusion.47) | copy-start | bytes 786436
  196.2 31.0 %collective-permute-start.5 = (f32[16,65,64]{1,2,0:T(8,128)}, f32[16,65,64]{1,2,0:T(8,128)S(1)}, u32[]{:S(2)}, u32[]{:S(2)}) collective-permute-start(f32[16,65,64]{1,2,0:T(8,128)} %pad_maximum_fusion.4), channel_id=1, source_target_pairs={{0,32},{4,36},{8,40},{12,44},{16,48},{20,52},{24,56},{28,60},{32,6... | collective-permute-start | bytes 798728 | tf_op jit(solution)/shard_map/ppermute | solution.py:16
  229.0 9.2 %copy-start.6 = (bf16[4,128,1024]{1,2,0:T(8,128)(2,1)S(1)}, bf16[4,128,1024]{1,2,0:T(8,128)(2,1)}, u32[]{:S(2)}) copy-start(bf16[4,128,1024]{1,2,0:T(8,128)(2,1)} %copy-done.5) | copy-start | bytes 3145732
  234.7 15.8 %collective-permute-start.6 = (f32[16,65,64]{1,2,0:T(8,128)S(1)}, f32[16,65,64]{1,2,0:T(8,128)S(1)}, u32[]{:S(2)}, u32[]{:S(2)}) collective-permute-start(f32[16,65,64]{1,2,0:T(8,128)S(1)} %pad_maximum_fusion.5), channel_id=1, source_target_pairs={{0,64},{4,68},{8,72},{12,76},{16,80},{20,84},{24,88},{28,92},{32,9... | collective-permute-start | bytes 798728 | tf_op jit(solution)/shard_map/ppermute | solution.py:16
  240.0 12.0 %copy-start.10 = (f32[16,64,64]{1,2,0:T(8,128)S(1)}, f32[16,64,64]{1,2,0:T(8,128)}, u32[]{:S(2)}) copy-start(f32[16,64,64]{1,2,0:T(8,128)} %copy-done.9) | copy-start | bytes 786436
  253.3 20.7 %collective-permute-start.7 = (f32[16,65,64]{1,2,0:T(8,128)S(1)}, f32[16,65,64]{1,2,0:T(8,128)S(1)}, u32[]{:S(2)}, u32[]{:S(2)}) collective-permute-start(f32[16,65,64]{1,2,0:T(8,128)S(1)} %pad_maximum_fusion.6), channel_id=1, source_target_pairs={{0,128},{4,132},{8,136},{12,140},{16,144},{20,148},{24,152},{28,15... | collective-permute-start | bytes 798728 | tf_op jit(solution)/shard_map/ppermute | solution.py:16
  276.1 10.3 %copy-start.4 = (f32[4,16,128,128]{3,2,1,0:T(8,128)S(1)}, f32[4,16,128,128]{3,2,1,0:T(8,128)}, u32[]{:S(2)}) copy-start(f32[4,16,128,128]{3,2,1,0:T(8,128)} %fusion.9) | copy-start | bytes 12582916
  276.1 10.3 %copy-start.7 = (f32[4,128,16,64]{1,3,2,0:T(8,128)S(1)}, f32[4,128,16,64]{1,3,2,0:T(8,128)}, u32[]{:S(2)}) copy-start(f32[4,128,16,64]{1,3,2,0:T(8,128)} %fusion) | copy-start | bytes 6291460
  (11 other events, 28.0 us)
